TPU v7x, 32 devices: a whole 2x2x4 slice. The times are simulated.
32 devices in a mesh: dp: 4 (over x, core), mp: 8 (over z, y).
Axes of the slice: x: 2, y: 2, z: 4, core: 2. Of those that a mesh axis runs over, the one named last changes fastest.
Arguments:
- queries: bfloat16 [512, 4096], P('dp'), may hold values from -103 to 103
- new_kv: bfloat16 [2, 512, 1024], P(None, 'dp'), may hold values from -6 to 6
- residual: bfloat16 [512, 4096], P('dp', 'mp'), may hold values from -2.4 to 2.4
- out_weight: bfloat16 [4096, 4096], P('mp'), may hold values from -0.125 to 0.125
- norm_gain: float32 [4096], replicated, may hold values from 0.5 to 1.5
- router: bfloat16 [4096, 8], replicated, may hold values from -0.09375 to 0.09375
- expert_in: bfloat16 [8, 2, 8192, 4096], P('dp', None, 'mp'), may hold values from -0.09375 to 0.09375
- expert_out: bfloat16 [8, 8192, 4096], P('dp', 'mp'), may hold values from -0.09375 to 0.09375
- node_cache: bfloat16 [2, 384, 8, 128, 128], P(None, 'dp', 'mp'), may hold values from -6 to 6
- leaf_cache: bfloat16 [2, 512, 8, 128, 128], P(None, 'dp', 'mp'), may hold values from -6 to 6
- slot_request: int32 [512], replicated, may hold values from 0 to 511, each once
- request_branch: int32 [512], replicated, may hold values from 0 to 31, as said below
- branch_parent: int32 [32], replicated, may hold values from 0 to 7, as said below
- root_owner: int32 [8], replicated, may hold values from 0 to 3, as said below
- branch_owner: int32 [32], replicated, may hold values from 0 to 3, as said below
- root_pages: int32 [8, 32], replicated, may hold values from 0 to 95, as said below
- branch_pages: int32 [32, 4], replicated, may hold values from 0 to 95, as said below
- root_len: int32 [8], replicated, may hold values from 1 to 4096, as said below
- branch_len: int32 [32], replicated, may hold values from 1 to 512
- leaf_len: int32 [512], P('dp'), may hold values from 1 to 128
- routes: int32 [512, 2], P('dp'), may hold values from 0 to 7, all different within a row; in each aligned block of 128 rows (0 to 127, 128 to 255, ...) at most 64 rows name the same one
Outputs:
- layer_out: bfloat16 [512, 4096], P('dp', 'mp')
Inputs may be any that keep to these rules, and one draw needn't show every extreme that they name: `request_branch`: at most 32 requests share a branch, and some branch has exactly 32. `branch_parent`: every root has exactly 4 branches. `root_owner`: every index of dp holds exactly 2 roots. `branch_owner`: every index of dp holds exactly 8 branches. `root_pages`: no slot of an owner's pool serves two pages of its nodes. `branch_pages`: no slot of an owner's pool serves two pages of its nodes. `root_len`: some root has 32 full pages.
All inputs are finite; a program needn't handle non-finite values.
Results may differ from a plain program's by a relative error of at most 0.034.
Values may be sent and summed in bfloat16 or wider, within the bound.
No kernel may reach another device: no remote copies, remote signals or barrier semaphores. Data moves between devices by JAX's collectives and lax.ppermute only.
A program may use at most 576 MiB of HBM per device.

v0:
```python
import jax
import jax.numpy as jnp
from jax import lax
from jax.sharding import PartitionSpec as P

HEADS = 32
KVH = 8
EXPERTS = 8
TOP = 2
PAGE = 128
ROOT_DEV = 2
BR_DEV = 8
BR_CAP = 32
E_CAP = 64


MASKED_SCORE = -1e30
NORM_EPS = 1e-05


def partner(x, axis, apart):
    return lax.ppermute(x, axis, [(i, i ^ 1 << apart) for i in range(lax.axis_size(axis))])


def merge_partials(first_part, second_part):
    first_sum, first_max, first_total = first_part
    second_sum, second_max, second_total = second_part
    common_max = jnp.maximum(first_max, second_max)
    first_factor = jnp.exp(first_max - common_max)
    second_factor = jnp.exp(second_max - common_max)
    merged_sum = first_sum * first_factor[..., None] + second_sum * second_factor[..., None]
    return (merged_sum, common_max, first_total * first_factor + second_total * second_factor)


def weigh_scores(scores, usable, values, pattern):
    masked_scores = jnp.where(usable, scores, MASKED_SCORE)
    row_max = jnp.max(masked_scores, axis=-1)
    weights = jnp.where(usable, jnp.exp(masked_scores - row_max[..., None]), 0.0)
    weight_total = jnp.sum(weights, axis=-1)
    weighted_sum = jnp.einsum(
        pattern, weights.astype(jnp.bfloat16), values, preferred_element_type=jnp.float32
    )
    return (weighted_sum, row_max, weight_total)


def node_partial(all_queries, members, page_pool, page_list, node_length, part_index):
    token_width = page_pool.shape[2]
    head_width = page_pool.shape[3]
    query_rows = jnp.take(all_queries, members, axis=0, mode="fill", fill_value=0)
    node_block = jnp.take(page_pool, page_list, axis=1)
    node_keys = node_block[0].reshape(-1, head_width)
    node_values = node_block[1].reshape(-1, head_width)
    positions = (
        jnp.arange(page_list.shape[0])[:, None] * PAGE
        + part_index * token_width
        + jnp.arange(token_width)[None, :]
    ).reshape(-1)
    usable = (positions < node_length)[None, None, :]
    scores = jnp.einsum(
        "sgd,ld->sgl", query_rows, node_keys, preferred_element_type=jnp.float32
    ) * head_width ** (-0.5)
    return weigh_scores(scores, usable, node_values, "sgl,ld->sgd")


def spread_rows(member_ids, partial_value, requests):
    weighted_sum, row_max, weight_total = partial_value
    flat_ids = member_ids.reshape(-1)
    groups = row_max.shape[-1]
    head_width = weighted_sum.shape[-1]
    sum_rows = (
        jnp.zeros((requests, groups, head_width), jnp.float32)
        .at[flat_ids]
        .set(weighted_sum.reshape(-1, groups, head_width), mode="drop")
    )
    max_rows = (
        jnp.zeros((requests, groups), jnp.float32)
        .at[flat_ids]
        .set(row_max.reshape(-1, groups), mode="drop")
    )
    total_rows = (
        jnp.zeros((requests, groups), jnp.float32)
        .at[flat_ids]
        .set(weight_total.reshape(-1, groups), mode="drop")
    )
    return (sum_rows, max_rows, total_rows)


def shards(
    queries,
    new_kv,
    residual,
    out_weight,
    norm_gain,
    router,
    expert_in,
    expert_out,
    node_cache,
    leaf_cache,
    slot_request,
    request_branch,
    branch_parent,
    root_owner,
    branch_owner,
    root_pages,
    branch_pages,
    root_len,
    branch_len,
    leaf_len,
    routes,
):
    head_width = node_cache.shape[-1]
    token_width = node_cache.shape[-2]
    part_count = lax.axis_size("mp") // KVH
    group_size = HEADS // KVH
    own_heads = HEADS // lax.axis_size("mp")
    local_rows = queries.shape[0]
    requests = slot_request.shape[0]
    branches = branch_parent.shape[0]
    root_count = root_owner.shape[0]
    kid_count = branches // root_count
    mp_index = lax.axis_index("mp")
    dp_index = lax.axis_index("dp")
    kv_head = mp_index // part_count
    part_index = mp_index % part_count
    group_queries = lax.dynamic_slice_in_dim(
        queries, kv_head * group_size * head_width, group_size * head_width, 1
    )
    all_queries = lax.all_gather(group_queries, "dp", axis=0, tiled=True).reshape(
        requests, group_size, head_width
    )
    slot_branch = jnp.take(request_branch, slot_request)
    branch_order = jnp.argsort(slot_branch, stable=True)
    branch_counts = jnp.sum(
        (slot_branch[None, :] == jnp.arange(branches)[:, None]).astype(jnp.int32), axis=1
    )
    branch_starts = jnp.cumsum(branch_counts) - branch_counts
    offsets = jnp.arange(BR_CAP)[None, :]
    spots = jnp.minimum(branch_starts[:, None] + offsets, requests - 1)
    members = jnp.where(offsets < branch_counts[:, None], jnp.take(branch_order, spots), requests)
    kids_of = jnp.argsort(branch_parent, stable=True).reshape(root_count, kid_count)
    page_pool = node_cache[:, :, 0]
    local_roots = jnp.nonzero(root_owner == dp_index, size=ROOT_DEV)[0]
    local_branches = jnp.nonzero(branch_owner == dp_index, size=BR_DEV)[0]

    def root_work(root_node):
        member_ids = jnp.take(members, kids_of[root_node], axis=0).reshape(-1)
        return (
            member_ids,
            node_partial(
                all_queries,
                member_ids,
                page_pool,
                root_pages[root_node],
                root_len[root_node],
                part_index,
            ),
        )

    def branch_work(branch_node):
        member_ids = members[branch_node]
        return (
            member_ids,
            node_partial(
                all_queries,
                member_ids,
                page_pool,
                branch_pages[branch_node],
                branch_len[branch_node],
                part_index,
            ),
        )

    root_ids, root_partial = jax.vmap(root_work)(local_roots)
    branch_ids, branch_partial = jax.vmap(branch_work)(local_branches)
    root_sum, root_max, root_total = spread_rows(root_ids, root_partial, requests)
    branch_sum, branch_max, branch_total = spread_rows(branch_ids, branch_partial, requests)
    returned = (
        lax.psum_scatter(root_sum, "dp", scatter_dimension=0, tiled=True),
        lax.psum_scatter(root_max, "dp", scatter_dimension=0, tiled=True),
        lax.psum_scatter(root_total, "dp", scatter_dimension=0, tiled=True),
        lax.psum_scatter(branch_sum, "dp", scatter_dimension=0, tiled=True),
        lax.psum_scatter(branch_max, "dp", scatter_dimension=0, tiled=True),
        lax.psum_scatter(branch_total, "dp", scatter_dimension=0, tiled=True),
    )
    leaf_block = leaf_cache[:, :, 0]
    mine_queries = group_queries.reshape(local_rows, group_size, head_width)
    leaf_places = part_index * token_width + jnp.arange(token_width)
    leaf_usable = (leaf_places[None, :] < leaf_len[:, None])[:, None, :]
    leaf_scores = jnp.einsum(
        "rgd,rtd->rgt", mine_queries, leaf_block[0], preferred_element_type=jnp.float32
    ) * head_width ** (-0.5)
    leaf_partial = weigh_scores(leaf_scores, leaf_usable, leaf_block[1], "rgt,rtd->rgd")
    running = merge_partials(
        (returned[0], returned[1], returned[2]), (returned[3], returned[4], returned[5])
    )
    running = merge_partials(running, leaf_partial)
    bit_count = part_count.bit_length() - 1
    for bit_index in reversed(range(bit_count)):
        half_heads = running[1].shape[1] // 2
        upper_side = mp_index >> bit_index & 1 == 1
        kept_half = tuple(
            (
                jnp.where(upper_side, component[:, half_heads:], component[:, :half_heads])
                for component in running
            )
        )
        sent_half = tuple(
            (
                jnp.where(upper_side, component[:, :half_heads], component[:, half_heads:])
                for component in running
            )
        )
        received = partner((sent_half[0], sent_half[1], sent_half[2]), "mp", bit_index)
        running = merge_partials(kept_half, received)
    own_queries = lax.dynamic_slice_in_dim(
        queries, mp_index * own_heads * head_width, own_heads * head_width, 1
    ).reshape(local_rows, own_heads, head_width)
    fresh_kv = lax.dynamic_slice_in_dim(new_kv, kv_head * head_width, head_width, 2)
    self_score = jnp.einsum(
        "rhd,rd->rh", own_queries, fresh_kv[0], preferred_element_type=jnp.float32
    ) * head_width ** (-0.5)
    weighted, row_max, weight_total = running
    common_max = jnp.maximum(row_max, self_score)
    old_factor = jnp.exp(row_max - common_max)
    new_factor = jnp.exp(self_score - common_max)
    weighted = (
        weighted * old_factor[..., None]
        + new_factor[..., None] * fresh_kv[1].astype(jnp.float32)[:, None, :]
    )
    weight_total = weight_total * old_factor + new_factor
    attended = (
        (weighted / weight_total[..., None])
        .astype(jnp.bfloat16)
        .reshape(local_rows, own_heads * head_width)
    )
    projected = jnp.dot(attended, out_weight, preferred_element_type=jnp.float32)
    slice_width = residual.shape[1]
    start_col = mp_index * slice_width
    own_cols = lax.dynamic_slice_in_dim(projected, start_col, slice_width, 1) + residual.astype(
        jnp.float32
    )
    projected = lax.dynamic_update_slice_in_dim(projected, own_cols, start_col, 1)
    hidden = lax.psum(projected.astype(jnp.bfloat16), "mp").astype(jnp.float32)
    inv_rms = lax.rsqrt(jnp.mean(hidden * hidden, axis=1) + NORM_EPS)
    normed = (hidden * inv_rms[:, None] * norm_gain[None, :]).astype(jnp.bfloat16)
    kept_cols = lax.dynamic_slice_in_dim(hidden, start_col, slice_width, 1)
    logits = jnp.dot(normed, router, preferred_element_type=jnp.float32)
    route_hits = routes[:, :, None] == jnp.arange(EXPERTS)[None, None, :]
    chosen = jnp.sum(jnp.where(route_hits, logits[:, None, :], 0.0), axis=2)
    gate_weights = jax.nn.softmax(chosen, axis=1)
    pair_experts = routes.reshape(-1)
    pair_onehot = (pair_experts[:, None] == jnp.arange(EXPERTS)[None, :]).astype(jnp.int32)
    pair_rank = jnp.sum((jnp.cumsum(pair_onehot, axis=0) - 1) * pair_onehot, axis=1)
    pair_slot = pair_experts * E_CAP + pair_rank
    slot_source = (
        jnp.full((EXPERTS * E_CAP,), local_rows, jnp.int32)
        .at[pair_slot]
        .set(jnp.arange(pair_experts.shape[0], dtype=jnp.int32) // TOP)
    )
    padded = jnp.concatenate([normed, jnp.zeros((1, normed.shape[1]), jnp.bfloat16)], axis=0)
    dp_count = lax.axis_size("dp")
    local_experts = expert_in.shape[0]
    outgoing = jnp.take(padded, slot_source, axis=0).reshape(
        dp_count, local_experts * E_CAP, normed.shape[1]
    )
    incoming = lax.all_to_all(outgoing, "dp", split_axis=0, concat_axis=0, tiled=True).reshape(
        dp_count, local_experts, E_CAP, normed.shape[1]
    )
    gate_up = jnp.einsum(
        "sjcd,jkfd->ksjcf", incoming, expert_in, preferred_element_type=jnp.float32
    )
    expert_hidden = (jax.nn.silu(gate_up[0]) * gate_up[1]).astype(jnp.bfloat16)
    expert_partial = jnp.einsum(
        "sjcf,jfd->sjcd", expert_hidden, expert_out, preferred_element_type=jnp.float32
    )
    summed = lax.psum_scatter(
        expert_partial.astype(jnp.bfloat16), "mp", scatter_dimension=3, tiled=True
    )
    returned_rows = lax.all_to_all(
        summed.reshape(dp_count, local_experts * E_CAP, slice_width),
        "dp",
        split_axis=0,
        concat_axis=0,
        tiled=True,
    )
    results = jnp.take(returned_rows.reshape(-1, slice_width), pair_slot, axis=0).reshape(
        local_rows, TOP, slice_width
    )
    layer_out = kept_cols + jnp.sum(gate_weights[:, :, None] * results.astype(jnp.float32), axis=1)
    return layer_out.astype(jnp.bfloat16)


def solution(mesh):
    placed = (
        P("dp", None),
        P(None, "dp", None),
        P("dp", "mp"),
        P("mp", None),
        P(),
        P(),
        P("dp", None, "mp", None),
        P("dp", "mp", None),
        P(None, "dp", "mp", None, None),
        P(None, "dp", "mp", None, None),
        P(),
        P(),
        P(),
        P(),
        P(),
        P(),
        P(),
        P(),
        P(),
        P("dp"),
        P("dp", None),
    )
    return jax.shard_map(
        shards, mesh=mesh, in_specs=placed, out_specs=P("dp", "mp"), check_vma=False
    )
```

profile of v0, /device:TPU:0, one launch (start us, length us, event | category | flops | bytes accessed | tf_op | source)
XLA Modules:
  0.0 496.7 jit_solution(14215773157432627096)
XLA Ops:
  6.5 0.7 fusion.84
  7.3 1.4 fusion.85
  8.8 0.6 scatter_custom_fusion
  9.6 2.3 sort.34
  12.0 0.7 shift-left_bitcast_fusion.1
  13.3 0.7 compare_select_fusion.11
  14.0 3.6 gather_fusion.1
  17.6 0.7 and_select_fusion.2
  18.8 3.8 sort.35
  22.6 6.9 %gather_fusion.2 = s32[1024]{0:T(1024)S(1)} fusion(s32[512]{0:T(512)S(1)} %get-tuple-element.8, s32[1024]{0:T(1024)S(1)} %broadcast_clamp_fusion), kind=kCustom, calls=%fused_computation.2 | custom fusion | bytes 12288 | tf_op jit(solution)/shard_map/jit(_take)/gather | solution.py:139
  31.3 8.6 %all_gather.3 = bf16[512,512]{1,0:T(8,128)(2,1)S(1)} all-gather(bf16[128,512]{1,0:T(8,128)(2,1)S(1)} %constant_dynamic-slice_fusion), channel_id=1, replica_groups=mesh['dp'=4,'mp'=8] {'dp'}, dimensions={0}, use_global_device_ids=true | all-gather | bytes 655360 | tf_op jit(solution)/shard_map/all_gather | solution.py:128
  40.0 1.0 gather_fusion.5
  41.1 5.8 %gather_fusion.7 = bf16[64,2,128,128]{3,2,1,0:T(8,128)(2,1)} fusion(bf16[2,96,128,128]{3,2,1,0:T(8,128)(2,1)} %bitcast.188, s32[1024]{0:T(1024)S(1)} %pad_clamp_fusion.5), kind=kCustom, calls=%fused_computation.7 | custom fusion | bytes 8388864 | tf_op jit(solution)/shard_map/vmap(jit(_take))/gather | solution.py:50
  46.9 2.6 fusion.18
  49.6 1.8 fusion.96
  51.5 0.6 gather_fusion.4
  52.2 3.0 fusion.4
  55.2 7.2 %fusion.5 = (f32[2,128,4]{1,2,0:T(4,128)S(1)}, bf16[2,128,4,4096]{3,1,2,0:T(8,128)(2,1)}) fusion(f32[2,128,4,4096]{3,1,2,0:T(8,128)S(1)} %get-tuple-element.35, f32[2,128,4]{1,2,0:T(4,128)S(1)} %get-tuple-element.34, pred[2,4096]{1,0:T(4,128)(4,1)S(1)} %broadcast_compare_fusion), kind=kLoop, calls=%fused_computation.31 | loop fusion | flops 25164800 | bytes 25182208 | tf_op jit(solution)/shard_map/vmap()/reduce_sum | solution.py:39
  62.6 1.8 scatter_custom_fusion.6
  64.5 0.6 fusion.87
  65.4 0.9 scatter_custom_fusion.3
  66.5 0.7 shift-left_bitcast_fusion
  69.1 1.0 gather_fusion.10
  70.4 3.8 gather_fusion.12
  75.9 0.6 gather_fusion.9
  76.6 0.6 fusion.27
  77.2 0.8 fusion.28
  78.2 1.8 scatter_custom_fusion.7
  80.2 1.8 scatter_custom_fusion.2
  82.3 1.8 scatter_custom_fusion.4
  84.2 6.3 %fusion.7 = f32[2,128,4,128]{3,1,0,2:T(8,128)S(1)} fusion(bf16[2,4096,128,1]{2,1,0,3:T(8,128)(2,1)} %bitcast.194, bf16[2,128,4,4096]{3,1,2,0:T(8,128)(2,1)} %get-tuple-element.23), kind=kOutput, calls=%fused_computation.33 | convolution fusion | flops 1073741824 | bytes 11010048 | tf_op jit(solution)/shard_map/vmap(sgl,ld->sgd)/dot_general | solution.py:40
  91.8 7.3 %scatter_fusion = f32[512,4,128]{2,1,0:T(4,128)S(1)} fusion(f32[512,4,128]{2,1,0:T(4,128)S(1)} %broadcast.675.clone.1, s32[256]{0:T(256)S(1)} %bitcast.213, f32[256,4,128]{2,1,0:T(4,128)S(1)} %copy.278), kind=kCustom, calls=%fused_computation.16 | custom fusion | bytes 1573888 | tf_op jit(solution)/shard_map/scatter | solution.py:73
  99.3 7.3 %scatter_fusion.1 = f32[512,4,128]{2,1,0:T(4,128)S(1)} fusion(f32[512,4,128]{2,1,0:T(4,128)S(1)} %broadcast.675.clone, s32[256]{0:T(256)S(1)} %bitcast.210, f32[256,4,128]{2,1,0:T(4,128)S(1)} %copy.293), kind=kCustom, calls=%fused_computation.20 | custom fusion | bytes 1573888 | tf_op jit(solution)/shard_map/scatter | solution.py:73
  106.6 1.0 copy-done.5
  108.0 4.5 fusion.98
  113.1 0.8 fusion.67
  114.2 0.6 dynamic-slice
  115.5 0.9 copy.339
  116.4 0.9 copy.341
  117.4 13.4 %reduce-scatter.16.cloned.1.call-done = f32[128,4]{1,0:T(8,128)} async-done(((f32[512,4]{1,0:T(8,128)}), f32[128,4]{1,0:T(8,128)}) %reduce-scatter.16.cloned.1.call-update) | async-done | bytes 2064
  130.7 0.9 copy.335
  131.6 21.7 %reduce-scatter.18.cloned.1.call-done = f32[128,4]{1,0:T(8,128)} async-done(((f32[512,4]{1,0:T(8,128)}), f32[128,4]{1,0:T(8,128)}) %reduce-scatter.18.cloned.1.call-update) | async-done | bytes 2064
  153.3 0.9 copy.337
  155.0 52.2 %all-reduce.11.cloned.1.call-done = (f32[512,4,128]{2,1,0:T(4,128)}, f32[512,4,128]{2,1,0:T(4,128)}) async-done(((f32[512,4,128]{2,1,0:T(4,128)}, f32[512,4,128]{2,1,0:T(4,128)}), (f32[512,4,128]{2,1,0:T(4,128)}, f32[512,4,128]{2,1,0:T(4,128)})) %all-reduce.11.cloned.1.call-update) | async-done | bytes 2097168
  207.1 3.3 fusion.41
  210.8 0.7 fusion.51
  211.6 1.1 convert_element_type.77
  212.8 1.4 scatter_custom_fusion.8
  214.2 76.9 %all-reduce.9.cloned.1.call-done = bf16[128,4096]{1,0:T(8,128)(2,1)} async-done(((bf16[128,4096]{1,0:T(8,128)(2,1)}), bf16[128,4096]{1,0:T(8,128)(2,1)}) %all-reduce.9.cloned.1.call-update) | async-done | bytes 1048592 | tf_op jit(solution)/shard_map/psum | solution.py:243
  291.1 1.5 multiply_reduce_fusion
  292.7 1.5 multiply_convert_fusion
  294.3 4.4 gather_fusion.13
  298.7 2.6 broadcast_select_fusion
  301.3 51.6 %all_to_all.10 = bf16[4,128,4096]{2,1,0:T(8,128)(2,1)} all-to-all(bf16[4,128,4096]{2,1,0:T(8,128)(2,1)S(1)} %broadcast_select_fusion), channel_id=1, replica_groups=mesh['dp'=4,'mp'=8] {'dp'}, dimensions={0} | all-to-all | bytes 8388608 | tf_op jit(solution)/shard_map/all_to_all | solution.py:266
  352.9 18.0 %fusion.19 = f32[2,4,2,64,1024]{4,3,0,1,2:T(8,128)} fusion(bf16[2,2,1024,4096]{3,2,1,0:T(8,128)(2,1)} %param.27, bf16[4,2,64,4096,1]{3,2,1,0,4:T(8,128)(2,1)} %bitcast.190), kind=kOutput, calls=%fused_computation.45 | convolution fusion | flops 8589934592 | bytes 41943040 | tf_op jit(solution)/shard_map/sjcd,jkfd->ksjcf/dot_general | solution.py:269
  370.9 13.6 %fusion.12 = bf16[4,2,64,4096]{3,2,0,1:T(8,128)(2,1)} fusion(bf16[2,1024,4096]{2,1,0:T(8,128)(2,1)} %param.28, f32[2,4,2,64,1024]{4,3,0,1,2:T(8,128)} %fusion.19), kind=kOutput, calls=%fused_computation.36 | convolution fusion | flops 4300210176 | bytes 25165824 | tf_op jit(solution)/shard_map/sjcf,jfd->sjcd/dot_general | solution.py:273
  385.7 86.1 %reduce-scatter.14.cloned.1.call-done = bf16[4,2,64,512]{3,2,0,1:T(8,128)(2,1)} async-done(((bf16[4,2,64,4096]{3,2,0,1:T(8,128)(2,1)}), bf16[4,2,64,512]{3,2,0,1:T(8,128)(2,1)}) %reduce-scatter.14.cloned.1.call-update) | async-done | bytes 524304 | tf_op jit(solution)/shard_map/reduce_scatter | solution.py:276
  471.8 1.9 copy.318
  473.7 3.6 all-to-all-start.1
  477.5 1.6 convert_element_type.78
  479.0 7.0 %all-to-all-done.1 = bf16[4,128,512]{2,1,0:T(8,128)(2,1)S(1)} async-done(((bf16[4,128,512]{2,1,0:T(8,128)(2,1)}), bf16[4,128,512]{2,1,0:T(8,128)(2,1)S(1)}, u32[]{:S(2)}, u32[]{:S(2)}) %all-to-all-start.1) | async-done | bytes 524320 | tf_op jit(solution)/shard_map/all_to_all | solution.py:279
  486.1 1.2 gather_fusion.14
  487.3 0.8 multiply_reduce_fusion.1
  488.2 1.6 add_convert_fusion
  (176 shorter events, 14.4 us)
Async XLA Ops:
  6.5 24.7 %copy-start = (bf16[128,4096]{1,0:T(8,128)(2,1)S(1)}, bf16[128,4096]{1,0:T(8,128)(2,1)}, u32[]{:S(2)}) copy-start(bf16[128,4096]{1,0:T(8,128)(2,1)} %param.21) | copy-start | bytes 3145732
  6.5 109.0 %reduce-scatter.20.cloned.1.call-start = ((), (), s32[]{:S(2)}) async-start(), calls=%async_computation.11 | async-start | bytes 327680
  22.6 7.9 %copy-start.12 = (s32[8,32]{1,0:T(8,128)S(1)}, s32[8,32]{1,0:T(8,128)}, u32[]{:S(2)}) copy-start(s32[8,32]{1,0:T(8,128)} %param.36) | copy-start | bytes 3076
  49.6 1.9 copy-start.2
  55.2 9.3 %copy-start.15 = (s32[32]{0:T(128)S(1)}, s32[32]{0:T(128)}, u32[]{:S(2)}) copy-start(s32[32]{0:T(128)} %param.35) | copy-start | bytes 388
  55.2 12.6 %copy-start.13 = (s32[32,4]{0,1:T(4,128)S(1)}, s32[32,4]{0,1:T(4,128)}, u32[]{:S(2)}) copy-start(s32[32,4]{0,1:T(4,128)} %param.37) | copy-start | bytes 1540
  55.2 13.4 %copy-start.11 = (s32[128,2]{0,1:T(2,128)S(1)}, s32[128,2]{0,1:T(2,128)}, u32[]{:S(2)}) copy-start(s32[128,2]{0,1:T(2,128)} %param.41) | copy-start | bytes 3076
  64.4 52.0 %reduce-scatter.22.cloned.1.call-start = ((), (), s32[]{:S(2)}) async-start(), calls=%async_computation.12 | async-start | bytes 327680
  74.2 1.7 copy-start.3
  80.0 50.7 %reduce-scatter.16.cloned.1.call-start = ((), (), s32[]{:S(2)}) async-start(), calls=%async_computation.9 | async-start | bytes 327680
  82.1 71.2 %reduce-scatter.18.cloned.1.call-start = ((), (), s32[]{:S(2)}) async-start(), calls=%async_computation.10 | async-start | bytes 327680
  84.1 123.0 %all-reduce.11.cloned.1.call-start = ((), (), s32[]{:S(2)}) async-start(), calls=%async_computation.13 | async-start | bytes 4194304
  91.3 16.6 %copy-start.14 = (s32[128]{0:T(128)S(1)}, s32[128]{0:T(128)}, u32[]{:S(2)}) copy-start(s32[128]{0:T(128)} %param.40) | copy-start | bytes 1540
  99.1 7.5 %copy-start.6 = (f32[512,4,128]{2,1,0:T(4,128)}, f32[512,4,128]{2,1,0:T(4,128)S(1)}, u32[]{:S(2)}) copy-start(f32[512,4,128]{2,1,0:T(4,128)S(1)} %scatter_fusion) | copy-start | bytes 3145732
  106.6 1.0 copy-start.5
  106.6 7.6 %copy-start.16 = (u32[32]{0:T(128)S(1)}, u32[32]{0:T(128)}, u32[]{:S(2)}) copy-start(u32[32]{0:T(128)} %constant.351) | copy-start | bytes 388
  107.6 183.5 %all-reduce.9.cloned.1.call-start = ((), (), s32[]{:S(2)}) async-start(), calls=%async_computation.7 | async-start | bytes 2097152 | tf_op jit(solution)/shard_map/psum | solution.py:243
  207.1 3.7 copy-start.7
  210.5 1.0 copy-start.8
  211.5 81.1 %copy-start.10 = (f32[4096]{0:T(1024)S(1)}, f32[4096]{0:T(1024)}, u32[]{:S(2)}) copy-start(f32[4096]{0:T(1024)} %param.25) | copy-start | bytes 49156
  212.7 259.0 %reduce-scatter.14.cloned.1.call-start = ((), (), s32[]{:S(2)}) async-start(), calls=%async_computation.8 | async-start | bytes 4718592 | tf_op jit(solution)/shard_map/reduce_scatter | solution.py:276
  384.5 0.8 copy-start.9
  384.5 93.0 %copy-start.4 = (bf16[128,4096]{1,0:T(8,128)(2,1)S(1)}, bf16[128,4096]{1,0:T(8,128)(2,1)}, u32[]{:S(2)}) copy-start(bf16[128,4096]{1,0:T(8,128)(2,1)} %all-reduce.9.cloned.1.call-done) | copy-start | bytes 3145732
  473.7 16.2 %copy-start.1 = (bf16[128,4096]{1,0:T(8,128)(2,1)S(1)}, bf16[128,4096]{1,0:T(8,128)(2,1)}, u32[]{:S(2)}) copy-start(bf16[128,4096]{1,0:T(8,128)(2,1)} %param.21) | copy-start | bytes 3145732
  473.7 12.4 %all-to-all-start.1 = ((bf16[4,128,512]{2,1,0:T(8,128)(2,1)}), bf16[4,128,512]{2,1,0:T(8,128)(2,1)S(1)}, u32[]{:S(2)}, u32[]{:S(2)}) async-start(bf16[4,128,512]{2,1,0:T(8,128)(2,1)} %bitcast.67), calls=%async_computation.2 | async-start | bytes 1048576 | tf_op jit(solution)/shard_map/all_to_all | solution.py:279
Sparse Core Ops, SparseCore 0:
  64.6 20.8 reduce-scatter.19
  88.1 20.0 reduce-scatter.21
  110.7 20.0 reduce-scatter.15
  133.2 20.0 reduce-scatter.17
  155.6 51.5 all-reduce.10
  212.9 78.2 all-reduce.8
  384.6 87.1 reduce-scatter.13
where the time goes:
time: 498 us; the launch traced here: 497 us
  waiting for transfers between devices  257 us (52%)
  local copies, waits for them, and re-layouts  70.4 us (14%)
  blocking collectives  60.2 us (12%)
  matrix products  51.1 us (10%)
  other arithmetic  38.7 us (8%)
  between operations  14.9 us (3%)
    unnamed x12, waiting for transfers between devices  87.3 us
    reduce_scatter x1, waiting for transfers between devices, shards(): lax.psum_scatter(expert_partial.astype(jnp.bfloat16), 'mp', scatter_dimen...  86.1 us
    psum x1, waiting for transfers between devices, shards(): hidden = lax.psum(projected.astype(jnp.bfloat16), 'mp').astype(jnp.float32)  76.9 us
    all_to_all x1, blocking collectives, shards(): lax.all_to_all(outgoing, 'dp', split_axis=0, concat_axis=0, tiled=True)  51.6 us
    dot_general x1, matrix products, shards(): jnp.einsum('sjcd,jkfd->ksjcf', incoming, expert_in, preferred_element_typ...  18 us
    scatter x2, local copies, waits for them, and re-layouts, spread_rows(): sum_rows = jnp.zeros((requests, groups, head_width), jnp.float32).at[flat...  14.6 us
    dot_general x1, matrix products, shards(): jnp.einsum('sjcf,jfd->sjcd', expert_hidden, expert_out, preferred_element...  13.6 us
    dot_general x3, matrix products, weigh_scores(): jnp.einsum(pattern, weights.astype(jnp.bfloat16), values, preferred_eleme...  10.1 us
  transfers between devices with their start and end apart: 8, of which 6 were waited for; matrix products, arithmetic and copies ran while one was open for 11% of the time, Pallas kernels for 0%

commit v1 on v0

--- a/solution.py
+++ b/solution.py
@@ -174,13 +174,34 @@
     branch_ids, branch_partial = jax.vmap(branch_work)(local_branches)
     root_sum, root_max, root_total = spread_rows(root_ids, root_partial, requests)
     branch_sum, branch_max, branch_total = spread_rows(branch_ids, branch_partial, requests)
+    groups = root_max.shape[1]
+    dp_count = lax.axis_size("dp")
+
+    def stat_row(row_max, row_total):
+        stats = jnp.concatenate([row_max, row_total], axis=1)
+        return jnp.pad(stats, ((0, 0), (0, head_width - 2 * groups)))[:, None, :]
+
+    packed = jnp.concatenate(
+        [root_sum, stat_row(root_max, root_total), branch_sum, stat_row(branch_max, branch_total)],
+        axis=1,
+    )
+    exchanged = lax.all_to_all(
+        packed.reshape(dp_count, local_rows, 2 * groups + 2, head_width),
+        "dp",
+        split_axis=0,
+        concat_axis=0,
+        tiled=True,
+    )
+    gathered = jnp.sum(exchanged, axis=0)
+    root_stats = gathered[:, groups]
+    branch_stats = gathered[:, 2 * groups + 1]
     returned = (
-        lax.psum_scatter(root_sum, "dp", scatter_dimension=0, tiled=True),
-        lax.psum_scatter(root_max, "dp", scatter_dimension=0, tiled=True),
-        lax.psum_scatter(root_total, "dp", scatter_dimension=0, tiled=True),
-        lax.psum_scatter(branch_sum, "dp", scatter_dimension=0, tiled=True),
-        lax.psum_scatter(branch_max, "dp", scatter_dimension=0, tiled=True),
-        lax.psum_scatter(branch_total, "dp", scatter_dimension=0, tiled=True),
+        gathered[:, :groups],
+        root_stats[:, :groups],
+        root_stats[:, groups : 2 * groups],
+        gathered[:, groups + 1 : 2 * groups + 1],
+        branch_stats[:, :groups],
+        branch_stats[:, groups : 2 * groups],
     )
     leaf_block = leaf_cache[:, :, 0]
     mine_queries = group_queries.reshape(local_rows, group_size, head_width)
@@ -258,7 +279,6 @@
         .set(jnp.arange(pair_experts.shape[0], dtype=jnp.int32) // TOP)
     )
     padded = jnp.concatenate([normed, jnp.zeros((1, normed.shape[1]), jnp.bfloat16)], axis=0)
-    dp_count = lax.axis_size("dp")
     local_experts = expert_in.shape[0]
     outgoing = jnp.take(padded, slot_source, axis=0).reshape(
         dp_count, local_experts * E_CAP, normed.shape[1]

time: 498 us -> 445 us (0.89)
  waiting for transfers between devices: 257 us -> 195 us
  other arithmetic: 38.7 us -> 45.7 us
    unnamed x12 -> x2, waiting for transfers between devices: 87.3 us -> 0.03 us
    all_to_all x0 -> x1, waiting for transfers between devices: none -> 25 us  [shards(): lax.all_to_all(packed.reshape(dp_count, local_rows, 2 * groups + 2, head_...]
    reduce_sum x3 -> x1, other arithmetic: 8.37 us -> 0.41 us  [weigh_scores(): weight_total = jnp.sum(weights, axis=-1)]
    convert_element_type x0 -> x2, other arithmetic: none -> 7.88 us  [weigh_scores(): weights.astype(jnp.bfloat16)]
  transfers between devices with their start and end apart: 8 -> 4, of which waited for: 6 -> 4; matrix products, arithmetic and copies ran while one was open for 11% -> 2% of each run, Pallas kernels for 0% -> 0%
where the time goes in v1:
time: 445 us; the launch traced here: 444 us
  waiting for transfers between devices  195 us (44%)
  local copies, waits for them, and re-layouts  70.6 us (16%)
  blocking collectives  60.4 us (14%)
  matrix products  49.6 us (11%)
  other arithmetic  45.7 us (10%)
  between operations  14.1 us (3%)
  starting transfers between devices  8.22 us (2%)
    reduce_scatter x1, waiting for transfers between devices, shards(): lax.psum_scatter(expert_partial.astype(jnp.bfloat16), 'mp', scatter_dimen...  86.1 us
    psum x1, waiting for transfers between devices, shards(): hidden = lax.psum(projected.astype(jnp.bfloat16), 'mp').astype(jnp.float32)  76.7 us
    all_to_all x1, blocking collectives, shards(): lax.all_to_all(outgoing, 'dp', split_axis=0, concat_axis=0, tiled=True)  51.6 us
    all_to_all x1, waiting for transfers between devices, shards(): lax.all_to_all(packed.reshape(dp_count, local_rows, 2 * groups + 2, head_...  25 us
    dot_general x1, matrix products, shards(): jnp.einsum('sjcd,jkfd->ksjcf', incoming, expert_in, preferred_element_typ...  18 us
    scatter x2, local copies, waits for them, and re-layouts, spread_rows(): sum_rows = jnp.zeros((requests, groups, head_width), jnp.float32).at[flat...  14.6 us
    dot_general x1, matrix products, shards(): jnp.einsum('sjcf,jfd->sjcd', expert_hidden, expert_out, preferred_element...  13.6 us
    gather x2, local copies, waits for them, and re-layouts, node_partial(): node_block = jnp.take(page_pool, page_list, axis=1)  9.53 us
  transfers between devices with their start and end apart: 4, of which 4 were waited for; matrix products, arithmetic and copies ran while one was open for 2% of the time, Pallas kernels for 0%

profile of v1, /device:TPU:0, one launch (start us, length us, event | category | flops | bytes accessed | tf_op | source)
XLA Modules:
  0.0 443.6 jit_solution(14719172141562675324)
XLA Ops:
  6.5 0.7 fusion.89
  7.3 1.4 fusion.90
  9.6 2.3 sort.34
  12.0 0.7 shift-left_bitcast_fusion.1
  13.3 0.7 compare_select_fusion.11
  14.0 3.6 gather_fusion.1
  17.6 0.7 and_select_fusion.2
  18.8 3.8 sort.35
  22.6 6.9 %gather_fusion.2 = s32[1024]{0:T(1024)S(1)} fusion(s32[512]{0:T(512)S(1)} %get-tuple-element.8, s32[1024]{0:T(1024)S(1)} %broadcast_clamp_fusion), kind=kCustom, calls=%fused_computation.2 | custom fusion | bytes 12288 | tf_op jit(solution)/shard_map/jit(_take)/gather | solution.py:139
  32.1 0.8 scatter_custom_fusion.4
  37.0 0.7 eq.80
  37.7 0.7 reshape.823
  39.0 8.8 %all_gather.3 = bf16[512,512]{1,0:T(8,128)(2,1)S(1)} all-gather(bf16[128,512]{1,0:T(8,128)(2,1)S(1)} %constant_dynamic-slice_fusion), channel_id=1, replica_groups=mesh['dp'=4,'mp'=8] {'dp'}, dimensions={0}, use_global_device_ids=true | all-gather | bytes 655360 | tf_op jit(solution)/shard_map/all_gather | solution.py:128
  47.9 1.0 gather_fusion.5
  49.0 5.8 %gather_fusion.7 = bf16[64,2,128,128]{3,2,1,0:T(8,128)(2,1)} fusion(bf16[2,96,128,128]{3,2,1,0:T(8,128)(2,1)} %bitcast.191, s32[1024]{0:T(1024)S(1)} %pad_clamp_fusion.5), kind=kCustom, calls=%fused_computation.7 | custom fusion | bytes 8388864 | tf_op jit(solution)/shard_map/vmap(jit(_take))/gather | solution.py:50
  54.8 2.6 fusion.18
  57.5 1.8 fusion.101
  60.1 3.0 fusion.4
  63.1 5.9 %fusion.6 = (bf16[2,128,4,4096]{3,1,2,0:T(8,128)(2,1)S(1)}, f32[2,128,4]{1,2,0:T(4,128)S(1)}) fusion(f32[2,128,4,4096]{3,1,2,0:T(8,128)S(1)} %get-tuple-element.37, f32[2,128,4]{1,2,0:T(4,128)S(1)} %get-tuple-element.36, pred[2,4096]{1,0:T(4,128)(4,1)S(1)} %broadcast_compare_fusion), kind=kLoop, calls=%fused_computation.32 | loop fusion | flops 25164800 | bytes 25182208 | tf_op jit(solution)/shard_map/vmap()/convert_element_type | solution.py:41
  69.0 2.3 fusion.7
  71.8 7.3 %scatter_fusion = f32[512,4,128]{2,1,0:T(4,128)S(1)} fusion(f32[512,4,128]{2,1,0:T(4,128)S(1)} %broadcast.679.clone.1, s32[256]{0:T(256)S(1)} %bitcast.218, f32[256,4,128]{2,1,0:T(4,128)S(1)} %copy.264), kind=kCustom, calls=%fused_computation.16 | custom fusion | bytes 1573888 | tf_op jit(solution)/shard_map/scatter | solution.py:73
  79.1 1.1 copy.285
  80.3 1.2 scatter_custom_fusion.3
  81.8 1.4 scatter_custom_fusion.2
  83.6 1.0 gather_fusion.10
  84.8 3.7 gather_fusion.12
  88.9 1.5 fusion.102
  91.2 1.8 fusion.27
  93.0 0.8 copy.323
  93.8 2.0 fusion.29
  95.8 0.8 copy.281
  96.6 0.7 fusion.73
  98.1 0.7 copy.308
  99.0 0.8 fusion.72
  100.4 1.2 scatter_custom_fusion.7
  101.7 1.6 scatter_custom_fusion.6
  103.6 1.7 fusion.37
  105.8 7.3 %scatter_fusion.1 = f32[512,4,128]{2,1,0:T(4,128)S(1)} fusion(f32[512,4,128]{2,1,0:T(4,128)S(1)} %broadcast.679.clone, s32[256]{0:T(256)S(1)} %bitcast.217, f32[256,4,128]{2,1,0:T(4,128)S(1)} %copy.278), kind=kCustom, calls=%fused_computation.20 | custom fusion | bytes 1573888 | tf_op jit(solution)/shard_map/scatter | solution.py:73
  113.4 1.7 pad_maximum_fusion
  115.1 4.5 %all-to-all-start = ((f32[4,128,10,128]{3,1,2,0:T(8,128)}), f32[4,128,10,128]{3,1,2,0:T(8,128)}, u32[]{:S(2)}, u32[]{:S(2)}) async-start(f32[4,128,10,128]{3,1,2,0:T(8,128)} %pad_maximum_fusion), calls=%async_computation | async-start | bytes 5242880 | tf_op jit(solution)/shard_map/all_to_all | solution.py:188
  119.8 4.5 %fusion.105 = (f32[128,4]{1,0:T(8,128)S(1)}, f32[128,4,128]{2,1,0:T(4,128)S(1)}) fusion(bf16[128,4,128]{2,1,0:T(4,128)(2,1)S(1)} %reshape.821, bf16[2,128,1,128,128]{4,3,1,2,0:T(8,128)(2,1)} %bitcast.223, pred[128,128]{1,0:T(8,128)(4,1)S(1)} %iota_compare_fusion), kind=kOutput, calls=%fused_computation.233 | convolution fusion | flops 16973312 | bytes 4605952 | tf_op jit(solution)/shard_map/rgd,rtd->rgt/dot_general | solution.py:210
  124.9 0.8 fusion.67
  126.0 25.0 %all-to-all-done = f32[4,128,10,128]{3,1,2,0:T(8,128)} async-done(((f32[4,128,10,128]{3,1,2,0:T(8,128)}), f32[4,128,10,128]{3,1,2,0:T(8,128)}, u32[]{:S(2)}, u32[]{:S(2)}) %all-to-all-start) | async-done | bytes 2621472 | tf_op jit(solution)/shard_map/all_to_all | solution.py:188
  151.0 2.0 reduce_sum.117
  154.1 3.3 fusion.41
  157.5 0.7 fusion.51
  158.3 1.1 convert_element_type.80
  159.5 1.7 scatter_custom_fusion.8
  161.3 76.7 %all-reduce.7.cloned.1.call-done = bf16[128,4096]{1,0:T(8,128)(2,1)} async-done(((bf16[128,4096]{1,0:T(8,128)(2,1)}), bf16[128,4096]{1,0:T(8,128)(2,1)}) %all-reduce.7.cloned.1.call-update) | async-done | bytes 1048592 | tf_op jit(solution)/shard_map/psum | solution.py:264
  238.0 1.5 multiply_reduce_fusion
  239.5 1.5 multiply_convert_fusion
  241.2 4.4 gather_fusion.13
  245.5 2.6 broadcast_select_fusion
  248.1 51.6 %all_to_all.15 = bf16[4,128,4096]{2,1,0:T(8,128)(2,1)} all-to-all(bf16[4,128,4096]{2,1,0:T(8,128)(2,1)S(1)} %broadcast_select_fusion), channel_id=1, replica_groups=mesh['dp'=4,'mp'=8] {'dp'}, dimensions={0} | all-to-all | bytes 8388608 | tf_op jit(solution)/shard_map/all_to_all | solution.py:286
  299.7 18.0 %fusion.19 = f32[2,4,2,64,1024]{4,3,0,1,2:T(8,128)} fusion(bf16[2,2,1024,4096]{3,2,1,0:T(8,128)(2,1)} %param.27, bf16[4,2,64,4096,1]{3,2,1,0,4:T(8,128)(2,1)} %bitcast.193), kind=kOutput, calls=%fused_computation.46 | convolution fusion | flops 8589934592 | bytes 41943040 | tf_op jit(solution)/shard_map/sjcd,jkfd->ksjcf/dot_general | solution.py:289
  317.7 13.6 %fusion.12 = bf16[4,2,64,4096]{3,2,0,1:T(8,128)(2,1)} fusion(bf16[2,1024,4096]{2,1,0:T(8,128)(2,1)} %param.28, f32[2,4,2,64,1024]{4,3,0,1,2:T(8,128)} %fusion.19), kind=kOutput, calls=%fused_computation.36 | convolution fusion | flops 4300210176 | bytes 25165824 | tf_op jit(solution)/shard_map/sjcf,jfd->sjcd/dot_general | solution.py:293
  332.5 86.1 %reduce-scatter.2.cloned.1.call-done = bf16[4,2,64,512]{3,2,0,1:T(8,128)(2,1)} async-done(((bf16[4,2,64,4096]{3,2,0,1:T(8,128)(2,1)}), bf16[4,2,64,512]{3,2,0,1:T(8,128)(2,1)}) %reduce-scatter.2.cloned.1.call-update) | async-done | bytes 524304 | tf_op jit(solution)/shard_map/reduce_scatter | solution.py:296
  418.7 1.9 copy.311
  420.5 3.6 all-to-all-start.2
  424.3 1.6 convert_element_type.81
  425.9 7.0 %all-to-all-done.2 = bf16[4,128,512]{2,1,0:T(8,128)(2,1)S(1)} async-done(((bf16[4,128,512]{2,1,0:T(8,128)(2,1)}), bf16[4,128,512]{2,1,0:T(8,128)(2,1)S(1)}, u32[]{:S(2)}, u32[]{:S(2)}) %all-to-all-start.2) | async-done | bytes 524320 | tf_op jit(solution)/shard_map/all_to_all | solution.py:299
  432.9 1.2 gather_fusion.14
  434.2 0.8 multiply_reduce_fusion.1
  435.1 1.6 add_convert_fusion
  (186 shorter events, 19.6 us)
Async XLA Ops:
  6.5 32.4 %copy-start = (bf16[128,4096]{1,0:T(8,128)(2,1)S(1)}, bf16[128,4096]{1,0:T(8,128)(2,1)}, u32[]{:S(2)}) copy-start(bf16[128,4096]{1,0:T(8,128)(2,1)} %param.21) | copy-start | bytes 3145732
  22.6 7.9 %copy-start.16 = (s32[8,32]{1,0:T(8,128)S(1)}, s32[8,32]{1,0:T(8,128)}, u32[]{:S(2)}) copy-start(s32[8,32]{1,0:T(8,128)} %param.36) | copy-start | bytes 3076
  22.6 8.6 %copy-start.21 = (s32[32]{0:T(128)S(1)}, s32[32]{0:T(128)}, u32[]{:S(2)}) copy-start(s32[32]{0:T(128)} %param.35) | copy-start | bytes 388
  22.6 12.3 %copy-start.18 = (s32[32,4]{0,1:T(4,128)S(1)}, s32[32,4]{0,1:T(4,128)}, u32[]{:S(2)}) copy-start(s32[32,4]{0,1:T(4,128)} %param.37) | copy-start | bytes 1540
  22.6 14.2 %copy-start.14 = (s32[128,2]{0,1:T(2,128)S(1)}, s32[128,2]{0,1:T(2,128)}, u32[]{:S(2)}) copy-start(s32[128,2]{0,1:T(2,128)} %param.41) | copy-start | bytes 3076
  47.9 6.9 %copy-start.7 = (bf16[512,4,128]{2,1,0:T(4,128)(2,1)}, bf16[512,4,128]{2,1,0:T(4,128)(2,1)S(1)}, u32[]{:S(2)}) copy-start(bf16[512,4,128]{2,1,0:T(4,128)(2,1)S(1)} %reshape.812) | copy-start | bytes 1572868
  57.5 1.9 copy-start.2
  63.0 5.9 %copy-start.9 = (bf16[2,1,32,128,128]{4,3,2,0,1:T(8,128)(2,1)S(1)}, bf16[2,1,32,128,128]{4,3,2,0,1:T(8,128)(2,1)}, u32[]{:S(2)}) copy-start(bf16[2,1,32,128,128]{4,3,2,0,1:T(8,128)(2,1)} %get-tuple-element.22) | copy-start | bytes 6291460
  71.3 12.3 %copy-start.8 = (bf16[512,4,128]{2,1,0:T(4,128)(2,1)S(1)}, bf16[512,4,128]{2,1,0:T(4,128)(2,1)}, u32[]{:S(2)}) copy-start(bf16[512,4,128]{2,1,0:T(4,128)(2,1)} %copy-done.7) | copy-start | bytes 1572868
  88.6 1.8 copy-start.20
  88.6 1.9 copy-start.3
  88.6 2.6 copy-start.17
  91.2 2.6 copy-start.12
  103.6 9.8 %copy-start.5 = (f32[4,128,4,128]{3,1,2,0:T(8,128)S(1)}, f32[4,128,4,128]{3,1,2,0:T(8,128)}, u32[]{:S(2)}) copy-start(f32[4,128,4,128]{3,1,2,0:T(8,128)} %copy.285) | copy-start | bytes 3145732
  113.4 6.4 %copy-start.19 = (s32[128]{0:T(128)S(1)}, s32[128]{0:T(128)}, u32[]{:S(2)}) copy-start(s32[128]{0:T(128)} %param.40) | copy-start | bytes 1540
  115.1 35.9 %all-to-all-start = ((f32[4,128,10,128]{3,1,2,0:T(8,128)}), f32[4,128,10,128]{3,1,2,0:T(8,128)}, u32[]{:S(2)}, u32[]{:S(2)}) async-start(f32[4,128,10,128]{3,1,2,0:T(8,128)} %pad_maximum_fusion), calls=%async_computation | async-start | bytes 5242880 | tf_op jit(solution)/shard_map/all_to_all | solution.py:188
  119.6 118.3 %all-reduce.7.cloned.1.call-start = ((), (), s32[]{:S(2)}) async-start(), calls=%async_computation.4 | async-start | bytes 2097152 | tf_op jit(solution)/shard_map/psum | solution.py:264
  154.1 3.4 copy-start.6
  157.3 0.9 copy-start.10
  158.3 81.2 %copy-start.13 = (f32[4096]{0:T(1024)S(1)}, f32[4096]{0:T(1024)}, u32[]{:S(2)}) copy-start(f32[4096]{0:T(1024)} %param.25) | copy-start | bytes 49156
  159.5 259.2 %reduce-scatter.2.cloned.1.call-start = ((), (), s32[]{:S(2)}) async-start(), calls=%async_computation.5 | async-start | bytes 4718592 | tf_op jit(solution)/shard_map/reduce_scatter | solution.py:296
  331.3 0.7 copy-start.15
  331.3 0.9 copy-start.11
  331.3 93.0 %copy-start.4 = (bf16[128,4096]{1,0:T(8,128)(2,1)S(1)}, bf16[128,4096]{1,0:T(8,128)(2,1)}, u32[]{:S(2)}) copy-start(bf16[128,4096]{1,0:T(8,128)(2,1)} %all-reduce.7.cloned.1.call-done) | copy-start | bytes 3145732
  420.5 16.2 %copy-start.1 = (bf16[128,4096]{1,0:T(8,128)(2,1)S(1)}, bf16[128,4096]{1,0:T(8,128)(2,1)}, u32[]{:S(2)}) copy-start(bf16[128,4096]{1,0:T(8,128)(2,1)} %param.21) | copy-start | bytes 3145732
  420.5 12.4 %all-to-all-start.2 = ((bf16[4,128,512]{2,1,0:T(8,128)(2,1)}), bf16[4,128,512]{2,1,0:T(8,128)(2,1)S(1)}, u32[]{:S(2)}, u32[]{:S(2)}) async-start(bf16[4,128,512]{2,1,0:T(8,128)(2,1)} %bitcast.73), calls=%async_computation.3 | async-start | bytes 1048576 | tf_op jit(solution)/shard_map/all_to_all | solution.py:299
Sparse Core Ops, SparseCore 0:
  159.6 78.3 all-reduce.6
  331.5 87.1 reduce-scatter.1

commit v2 on v1

--- a/solution.py
+++ b/solution.py
@@ -41,48 +41,6 @@
         pattern, weights.astype(jnp.bfloat16), values, preferred_element_type=jnp.float32
     )
     return (weighted_sum, row_max, weight_total)
-
-
-def node_partial(all_queries, members, page_pool, page_list, node_length, part_index):
-    token_width = page_pool.shape[2]
-    head_width = page_pool.shape[3]
-    query_rows = jnp.take(all_queries, members, axis=0, mode="fill", fill_value=0)
-    node_block = jnp.take(page_pool, page_list, axis=1)
-    node_keys = node_block[0].reshape(-1, head_width)
-    node_values = node_block[1].reshape(-1, head_width)
-    positions = (
-        jnp.arange(page_list.shape[0])[:, None] * PAGE
-        + part_index * token_width
-        + jnp.arange(token_width)[None, :]
-    ).reshape(-1)
-    usable = (positions < node_length)[None, None, :]
-    scores = jnp.einsum(
-        "sgd,ld->sgl", query_rows, node_keys, preferred_element_type=jnp.float32
-    ) * head_width ** (-0.5)
-    return weigh_scores(scores, usable, node_values, "sgl,ld->sgd")
-
-
-def spread_rows(member_ids, partial_value, requests):
-    weighted_sum, row_max, weight_total = partial_value
-    flat_ids = member_ids.reshape(-1)
-    groups = row_max.shape[-1]
-    head_width = weighted_sum.shape[-1]
-    sum_rows = (
-        jnp.zeros((requests, groups, head_width), jnp.float32)
-        .at[flat_ids]
-        .set(weighted_sum.reshape(-1, groups, head_width), mode="drop")
-    )
-    max_rows = (
-        jnp.zeros((requests, groups), jnp.float32)
-        .at[flat_ids]
-        .set(row_max.reshape(-1, groups), mode="drop")
-    )
-    total_rows = (
-        jnp.zeros((requests, groups), jnp.float32)
-        .at[flat_ids]
-        .set(weight_total.reshape(-1, groups), mode="drop")
-    )
-    return (sum_rows, max_rows, total_rows)
 
 
 def shards(
@@ -117,7 +75,6 @@
     requests = slot_request.shape[0]
     branches = branch_parent.shape[0]
     root_count = root_owner.shape[0]
-    kid_count = branches // root_count
     mp_index = lax.axis_index("mp")
     dp_index = lax.axis_index("dp")
     kv_head = mp_index // part_count
@@ -129,62 +86,66 @@
         requests, group_size, head_width
     )
     slot_branch = jnp.take(request_branch, slot_request)
-    branch_order = jnp.argsort(slot_branch, stable=True)
-    branch_counts = jnp.sum(
-        (slot_branch[None, :] == jnp.arange(branches)[:, None]).astype(jnp.int32), axis=1
-    )
-    branch_starts = jnp.cumsum(branch_counts) - branch_counts
-    offsets = jnp.arange(BR_CAP)[None, :]
-    spots = jnp.minimum(branch_starts[:, None] + offsets, requests - 1)
-    members = jnp.where(offsets < branch_counts[:, None], jnp.take(branch_order, spots), requests)
-    kids_of = jnp.argsort(branch_parent, stable=True).reshape(root_count, kid_count)
-    page_pool = node_cache[:, :, 0]
+    slot_root = jnp.take(branch_parent, slot_branch)
     local_roots = jnp.nonzero(root_owner == dp_index, size=ROOT_DEV)[0]
     local_branches = jnp.nonzero(branch_owner == dp_index, size=BR_DEV)[0]
-
-    def root_work(root_node):
-        member_ids = jnp.take(members, kids_of[root_node], axis=0).reshape(-1)
-        return (
-            member_ids,
-            node_partial(
-                all_queries,
-                member_ids,
-                page_pool,
-                root_pages[root_node],
-                root_len[root_node],
-                part_index,
-            ),
-        )
-
-    def branch_work(branch_node):
-        member_ids = members[branch_node]
-        return (
-            member_ids,
-            node_partial(
-                all_queries,
-                member_ids,
-                page_pool,
-                branch_pages[branch_node],
-                branch_len[branch_node],
-                part_index,
-            ),
-        )
-
-    root_ids, root_partial = jax.vmap(root_work)(local_roots)
-    branch_ids, branch_partial = jax.vmap(branch_work)(local_branches)
-    root_sum, root_max, root_total = spread_rows(root_ids, root_partial, requests)
-    branch_sum, branch_max, branch_total = spread_rows(branch_ids, branch_partial, requests)
-    groups = root_max.shape[1]
+    page_pool = node_cache[:, :, 0]
+    pool_pages = page_pool.shape[1]
+    flat_queries = all_queries.reshape(requests, group_size * head_width)
+
+    def selection(node_of_slot, nodes, cap):
+        hit = node_of_slot[None, :] == nodes[:, None]
+        rank = jnp.cumsum(hit.astype(jnp.int32), axis=1) - 1
+        return hit[:, None, :] & (rank[:, None, :] == jnp.arange(cap)[None, :, None])
+
+    def level_rows(nodes, node_pages, node_len, cap):
+        pick = selection(node_of_slot_for[cap], nodes, cap)
+        member_queries = jnp.einsum(
+            "nks,sx->nkx", pick.astype(jnp.bfloat16), flat_queries,
+            preferred_element_type=jnp.float32,
+        ).astype(jnp.bfloat16).reshape(nodes.shape[0], cap, group_size, head_width)
+        page_pick = (
+            jnp.take(node_pages, nodes, axis=0)[:, :, None] == jnp.arange(pool_pages)[None, None, :]
+        ).astype(jnp.bfloat16)
+        blocks = jnp.einsum(
+            "npq,cqtd->cnptd", page_pick, page_pool, preferred_element_type=jnp.float32
+        ).astype(jnp.bfloat16)
+        lengths = jnp.take(node_len, nodes)
+
+        def one_node(queries_of, keys_of, values_of, length):
+            page_count = keys_of.shape[0]
+            positions = (
+                jnp.arange(page_count)[:, None] * PAGE
+                + part_index * token_width
+                + jnp.arange(token_width)[None, :]
+            ).reshape(-1)
+            usable = (positions < length)[None, None, :]
+            scores = jnp.einsum(
+                "sgd,ld->sgl", queries_of, keys_of.reshape(-1, head_width),
+                preferred_element_type=jnp.float32,
+            ) * head_width ** (-0.5)
+            return weigh_scores(scores, usable, values_of.reshape(-1, head_width), "sgl,ld->sgd")
+
+        weighted_sum, row_max, weight_total = jax.vmap(one_node)(
+            member_queries, blocks[0], blocks[1], lengths
+        )
+        stats = jnp.concatenate([row_max, weight_total], axis=2)
+        stats = jnp.pad(stats, ((0, 0), (0, 0), (0, head_width - 2 * group_size)))
+        rows = jnp.concatenate(
+            [weighted_sum.reshape(nodes.shape[0], cap, group_size * head_width), stats], axis=2
+        )
+        return jnp.einsum(
+            "nks,nkc->sc", pick.astype(jnp.float32), rows,
+            precision=lax.Precision.HIGHEST, preferred_element_type=jnp.float32,
+        )
+
+    root_cap = (branches // root_count) * BR_CAP
+    node_of_slot_for = {root_cap: slot_root, BR_CAP: slot_branch}
+    root_rows = level_rows(local_roots, root_pages, root_len, root_cap)
+    branch_rows = level_rows(local_branches, branch_pages, branch_len, BR_CAP)
+    groups = group_size
     dp_count = lax.axis_size("dp")
-
-    def stat_row(row_max, row_total):
-        stats = jnp.concatenate([row_max, row_total], axis=1)
-        return jnp.pad(stats, ((0, 0), (0, head_width - 2 * groups)))[:, None, :]
-
-    packed = jnp.concatenate(
-        [root_sum, stat_row(root_max, root_total), branch_sum, stat_row(branch_max, branch_total)],
-        axis=1,
-    )
+    packed = jnp.concatenate([root_rows, branch_rows], axis=1)
     exchanged = lax.all_to_all(
         packed.reshape(dp_count, local_rows, 2 * groups + 2, head_width),
         "dp",
@@ -256,15 +217,23 @@
     )
     projected = jnp.dot(attended, out_weight, preferred_element_type=jnp.float32)
     slice_width = residual.shape[1]
+    mp_count = lax.axis_size("mp")
     start_col = mp_index * slice_width
     own_cols = lax.dynamic_slice_in_dim(projected, start_col, slice_width, 1) + residual.astype(
         jnp.float32
     )
     projected = lax.dynamic_update_slice_in_dim(projected, own_cols, start_col, 1)
-    hidden = lax.psum(projected.astype(jnp.bfloat16), "mp").astype(jnp.float32)
+    terms = projected.astype(jnp.bfloat16).reshape(local_rows, mp_count, slice_width)
+    terms = jnp.transpose(terms, (1, 0, 2))
+    received_terms = lax.all_to_all(terms, "mp", split_axis=0, concat_axis=0, tiled=True)
+    kept_cols = jnp.sum(received_terms.astype(jnp.float32), axis=0)
+    spread_cols = jnp.broadcast_to(
+        kept_cols.astype(jnp.bfloat16)[None], (mp_count, local_rows, slice_width)
+    )
+    all_cols = lax.all_to_all(spread_cols, "mp", split_axis=0, concat_axis=0, tiled=True)
+    hidden = jnp.transpose(all_cols, (1, 0, 2)).reshape(local_rows, -1).astype(jnp.float32)
     inv_rms = lax.rsqrt(jnp.mean(hidden * hidden, axis=1) + NORM_EPS)
     normed = (hidden * inv_rms[:, None] * norm_gain[None, :]).astype(jnp.bfloat16)
-    kept_cols = lax.dynamic_slice_in_dim(hidden, start_col, slice_width, 1)
     logits = jnp.dot(normed, router, preferred_element_type=jnp.float32)
     route_hits = routes[:, :, None] == jnp.arange(EXPERTS)[None, None, :]
     chosen = jnp.sum(jnp.where(route_hits, logits[:, None, :], 0.0), axis=2)

time: 445 us -> 422 us (0.948)
  waiting for transfers between devices: 195 us -> 144 us
  local copies, waits for them, and re-layouts: 70.6 us -> 38 us
  blocking collectives: 60.4 us -> 92.2 us
  matrix products: 49.6 us -> 66.1 us
  other arithmetic: 45.7 us -> 50.8 us
    psum x1 -> x0, waiting for transfers between devices: 76.7 us -> none  [shards(): hidden = lax.psum(projected.astype(jnp.bfloat16), 'mp').astype(jnp.float32)]
    all_to_all x0 -> x1, blocking collectives: none -> 31.3 us  [shards(): lax.all_to_all(terms, 'mp', split_axis=0, concat_axis=0, tiled=True)]
    all_to_all x0 -> x1, waiting for transfers between devices: none -> 25.5 us  [shards(): lax.all_to_all(spread_cols, 'mp', split_axis=0, concat_axis=0, tiled=True)]
    scatter x10 -> x0, local copies, waits for them, and re-layouts: 20.5 us -> none  [the longest x2 14.6 us: spread_rows(): sum_rows = jnp.zeros((requests, groups, head_width), jnp.float32).at[flat...]
    select_n x13 -> x6, other arithmetic: 4.51 us -> 22.9 us  [the longest x1 20.7 us: shards(): slot_root = jnp.take(branch_parent, slot_branch)]
    gather x16 -> x6, local copies, waits for them, and re-layouts: 22.7 us -> 6.96 us  [the longest x2 3.91 us: shards(): slot_root = jnp.take(branch_parent, slot_branch)]
    dot_general x2 -> x8, matrix products: 4.78 us -> 20.5 us  [the longest x2 14.1 us: level_rows(): jnp.einsum('npq,cqtd->cnptd', page_pick, page_pool, preferred_element_typ...]
    convert_element_type x4, other arithmetic: 10.6 us -> 0.28 us  [the longest x2 0.14 us: selection(): rank = jnp.cumsum(hit.astype(jnp.int32), axis=1) - 1]
where the time goes in v2:
time: 422 us; the launch traced here: 418 us
  waiting for transfers between devices  144 us (34%)
  blocking collectives  92.2 us (22%)
  matrix products  66.1 us (16%)
  other arithmetic  50.8 us (12%)
  local copies, waits for them, and re-layouts  38 us (9%)
  between operations  14.2 us (3%)
  starting transfers between devices  11.7 us (3%)
    reduce_scatter x1, waiting for transfers between devices, shards(): lax.psum_scatter(expert_partial.astype(jnp.bfloat16), 'mp', scatter_dimen...  85.3 us
    all_to_all x1, blocking collectives, shards(): lax.all_to_all(outgoing, 'dp', split_axis=0, concat_axis=0, tiled=True)  51.8 us
    all_to_all x1, blocking collectives, shards(): lax.all_to_all(terms, 'mp', split_axis=0, concat_axis=0, tiled=True)  31.3 us
    all_to_all x1, waiting for transfers between devices, shards(): lax.all_to_all(spread_cols, 'mp', split_axis=0, concat_axis=0, tiled=True)  25.5 us
    all_to_all x1, waiting for transfers between devices, shards(): lax.all_to_all(packed.reshape(dp_count, local_rows, 2 * groups + 2, head_...  25 us
    select_n x1, other arithmetic, shards(): slot_root = jnp.take(branch_parent, slot_branch)  20.7 us
    dot_general x1, matrix products, shards(): jnp.einsum('sjcd,jkfd->ksjcf', incoming, expert_in, preferred_element_typ...  18 us
    dot_general x2, matrix products, level_rows(): jnp.einsum('npq,cqtd->cnptd', page_pick, page_pool, preferred_element_typ...  14.1 us
  transfers between devices with their start and end apart: 4, of which 4 were waited for; matrix products, arithmetic and copies ran while one was open for 2% of the time, Pallas kernels for 0%

profile of v2, /device:TPU:0, one launch (start us, length us, event | category | flops | bytes accessed | tf_op | source)
XLA Modules:
  0.0 417.6 jit_solution(3147235901397206229)
XLA Ops:
  6.5 2.1 fusion.156
  8.6 1.8 fusion.157
  10.5 0.8 copy.237
  11.5 0.7 broadcast_multiply_fusion
  12.2 0.7 fusion.131
  12.9 1.3 fusion.132
  14.2 0.7 fusion.129
  14.8 1.4 fusion.130
  16.2 0.6 reduce-window.48
  17.4 1.4 scatter_custom_fusion.2
  18.8 0.7 compare_select_fusion.2
  19.8 0.8 scatter_custom_fusion.1
  20.9 0.7 fusion.126
  21.6 0.6 scatter_custom_fusion
  22.4 0.7 fusion.127
  23.1 1.3 gather_fusion.1
  24.4 0.7 broadcast_select_fusion.5
  25.1 3.6 gather_fusion
  28.7 20.7 %select_select_fusion = (s32[512]{0:T(512)S(1)}, s32[512]{0:T(512)S(1)}) fusion(s32[]{:T(128)} %bitcast, s32[]{:T(128)} %bitcast.1, s32[]{:T(128)} %bitcast.2, s32[]{:T(128)} %bitcast.3, s32[]{:T(128)} %bitcast.4, s32[]{:T(128)} %bitcast.5, s32[]{:T(128)} %bitcast.6, s32[]{:T(128)} %bitcast.7, s32[]{:T(128)} %bitcast.8, s32[]{:T(128)} %bitcast.9, ...), kind=kLoop, calls=%fused_computation.195 | loop fusion | flops 38912 | bytes 8320 | tf_op jit(solution)/shard_map/jit(_take)/select_n | solution.py:89
  49.6 0.6 reduce-window.31
  50.7 9.1 %all_gather.3 = bf16[512,512]{1,0:T(8,128)(2,1)S(1)} all-gather(bf16[128,512]{1,0:T(8,128)(2,1)S(1)} %constant_dynamic-slice_fusion), channel_id=1, replica_groups=mesh['dp'=4,'mp'=8] {'dp'}, dimensions={0}, use_global_device_ids=true | all-gather | bytes 655360 | tf_op jit(solution)/shard_map/all_gather | solution.py:85
  60.5 7.4 %convert_bitcast_fusion = bf16[2,2,32,128,128]{4,2,3,0,1:T(8,128)(2,1)S(1)} fusion(bf16[2,96,128,128]{3,2,1,0:T(8,128)(2,1)} %bitcast.256, s32[2,32]{1,0:T(2,128)S(1)} %broadcast_select_fusion.3), kind=kOutput, calls=%fused_computation.34 | convolution fusion | flops 404756480 | bytes 10486016 | tf_op jit(solution)/shard_map/npq,cqtd->cnptd/dot_general | solution.py:110
  67.9 0.7 fusion.153
  68.6 0.8 copy.202
  69.5 0.8 copy.204
  70.4 0.7 fusion.40
  71.1 2.8 fusion.4
  73.9 5.1 %fusion.5 = f32[2,128,4]{1,2,0:T(4,128)S(1)} fusion(f32[2,128,4,4096]{3,1,2,0:T(8,128)S(1)} %get-tuple-element.65, f32[2,128,4]{1,2,0:T(4,128)S(1)} %get-tuple-element.64, pred[2,4096]{1,0:T(4,128)(4,1)S(1)} %broadcast_compare_fusion), kind=kLoop, calls=%fused_computation.17 | loop fusion | flops 20970496 | bytes 16793600 | tf_op jit(solution)/shard_map/vmap()/reduce_sum | solution.py:39
  79.0 4.2 %fusion.7 = f32[2,128,4,128]{1,3,2,0:T(8,128)S(1)} fusion(bf16[2,4096,128,1]{2,1,3,0:T(8,128)(2,1)S(1)} %bitcast.262, f32[2,128,4,4096]{3,1,2,0:T(8,128)S(1)} %get-tuple-element.65, f32[2,128,4]{1,2,0:T(4,128)S(1)} %get-tuple-element.64, pred[2,4096]{1,0:T(4,128)(4,1)S(1)} %broadcast_compare_fusion), kind=kOutput, calls=%fused_computation.19 | convolution fusion | flops 1094713344 | bytes 19410944 | tf_op jit(solution)/shard_map/vmap(sgl,ld->sgd)/dot_general | solution.py:40
  83.6 0.6 gather_fusion.3
  84.2 0.7 broadcast_select_fusion.4
  85.1 1.1 reduce-window.36
  87.3 6.8 %convert_bitcast_fusion.2 = bf16[2,8,4,128,128]{4,1,3,0,2:T(8,128)(2,1)S(1)} fusion(bf16[2,96,128,128]{3,2,1,0:T(8,128)(2,1)} %bitcast.257, s32[8,4]{0,1:T(4,128)S(1)} %copy.210), kind=kOutput, calls=%fused_computation.49 | convolution fusion | flops 202378240 | bytes 8388736 | tf_op jit(solution)/shard_map/npq,cqtd->cnptd/dot_general | solution.py:110
  94.7 0.6 fusion.37
  95.3 0.7 fusion.38
  96.0 0.8 convolution_bitcast_fusion.2
  97.0 1.0 convolution_bitcast_fusion.1
  98.0 0.9 convolution_bitcast_fusion
  98.9 1.7 pad_maximum_fusion
  100.7 4.6 %reshape.818 = f32[4,128,10,128]{3,2,1,0:T(8,128)} reshape(f32[512,1280]{1,0:T(8,128)} %pad_maximum_fusion) | data formatting | bytes 5242880 | tf_op jit(solution)/shard_map/reshape | solution.py:150
  105.2 4.7 %copy.218 = f32[4,128,10,128]{1,3,2,0:T(8,128)} copy(f32[4,128,10,128]{3,2,1,0:T(8,128)} %reshape.818) | data formatting | bytes 5242880 | tf_op jit(solution)/shard_map/reshape | solution.py:150
  110.0 4.7 %all-to-all-start = ((f32[4,128,10,128]{1,3,2,0:T(8,128)}), f32[4,128,10,128]{1,3,2,0:T(8,128)}, u32[]{:S(2)}, u32[]{:S(2)}) async-start(f32[4,128,10,128]{1,3,2,0:T(8,128)} %copy.218), calls=%async_computation | async-start | bytes 5242880 | tf_op jit(solution)/shard_map/all_to_all | solution.py:149
  114.8 4.5 %fusion.158 = (f32[128,4]{1,0:T(8,128)S(1)}, f32[128,4,128]{2,1,0:T(4,128)S(1)}) fusion(bf16[128,4,128]{2,1,0:T(4,128)(2,1)S(1)} %reshape.670, bf16[2,128,1,128,128]{4,3,1,2,0:T(8,128)(2,1)} %bitcast.275, pred[128,128]{1,0:T(8,128)(4,1)S(1)} %iota_compare_fusion.6), kind=kOutput, calls=%fused_computation.270 | convolution fusion | flops 16973312 | bytes 4605952 | tf_op jit(solution)/shard_map/rgd,rtd->rgt/dot_general | solution.py:171
  119.9 0.8 fusion.101
  121.0 25.0 %all-to-all-done = f32[4,128,10,128]{1,3,2,0:T(8,128)} async-done(((f32[4,128,10,128]{1,3,2,0:T(8,128)}), f32[4,128,10,128]{1,3,2,0:T(8,128)}, u32[]{:S(2)}, u32[]{:S(2)}) %all-to-all-start) | async-done | bytes 2621472 | tf_op jit(solution)/shard_map/all_to_all | solution.py:149
  146.0 2.0 reduce_sum.116
  149.2 3.2 fusion.60
  152.6 0.7 fusion.93
  153.7 31.3 %all_to_all.25 = bf16[8,128,512]{2,1,0:T(8,128)(2,1)S(1)} all-to-all(bf16[8,128,512]{2,1,0:T(8,128)(2,1)S(1)} %bitcast.260), channel_id=1, replica_groups=mesh['dp'=4,'mp'=8] {'mp'}, dimensions={0} | all-to-all | bytes 2097152 | tf_op jit(solution)/shard_map/all_to_all | solution.py:228
  185.1 1.1 broadcast_in_dim.215
  186.2 3.6 all-to-all-start.2
  189.8 25.5 %all-to-all-done.2 = bf16[8,128,512]{2,1,0:T(8,128)(2,1)S(1)} async-done(((bf16[8,128,512]{2,1,0:T(8,128)(2,1)}), bf16[8,128,512]{2,1,0:T(8,128)(2,1)S(1)}, u32[]{:S(2)}, u32[]{:S(2)}) %all-to-all-start.2) | async-done | bytes 1048608 | tf_op jit(solution)/shard_map/all_to_all | solution.py:233
  216.5 4.4 %gather_fusion.5 = bf16[512,4096]{1,0:T(8,128)(2,1)} fusion(bf16[129,4096]{1,0:T(8,128)(2,1)S(1)} %concatenate.23, s32[1024]{0:T(1024)S(1)} %pad_clamp_fusion.1), kind=kCustom, calls=%fused_computation.5 | custom fusion | bytes 8390656 | tf_op jit(solution)/shard_map/jit(_take)/gather | solution.py:252
  220.9 2.6 broadcast_select_fusion
  223.5 51.8 %all_to_all.26 = bf16[4,128,4096]{2,1,0:T(8,128)(2,1)} all-to-all(bf16[4,128,4096]{2,1,0:T(8,128)(2,1)S(1)} %broadcast_select_fusion), channel_id=1, replica_groups=mesh['dp'=4,'mp'=8] {'dp'}, dimensions={0} | all-to-all | bytes 8388608 | tf_op jit(solution)/shard_map/all_to_all | solution.py:255
  275.4 18.0 %fusion.27 = f32[2,4,2,64,1024]{4,3,0,1,2:T(8,128)} fusion(bf16[2,2,1024,4096]{3,2,1,0:T(8,128)(2,1)} %param.27, bf16[4,2,64,4096,1]{3,2,1,0,4:T(8,128)(2,1)} %bitcast.259), kind=kOutput, calls=%fused_computation.39 | convolution fusion | flops 8589934592 | bytes 41943040 | tf_op jit(solution)/shard_map/sjcd,jkfd->ksjcf/dot_general | solution.py:258
  293.3 13.6 %fusion.19 = bf16[4,2,64,4096]{3,2,0,1:T(8,128)(2,1)} fusion(bf16[2,1024,4096]{2,1,0:T(8,128)(2,1)} %param.28, f32[2,4,2,64,1024]{4,3,0,1,2:T(8,128)} %fusion.27), kind=kOutput, calls=%fused_computation.28 | convolution fusion | flops 4300210176 | bytes 25165824 | tf_op jit(solution)/shard_map/sjcf,jfd->sjcd/dot_general | solution.py:262
  308.2 85.3 %reduce-scatter.2.cloned.1.call-done = bf16[4,2,64,512]{3,2,0,1:T(8,128)(2,1)} async-done(((bf16[4,2,64,4096]{3,2,0,1:T(8,128)(2,1)}), bf16[4,2,64,512]{3,2,0,1:T(8,128)(2,1)}) %reduce-scatter.2.cloned.1.call-update) | async-done | bytes 524304 | tf_op jit(solution)/shard_map/reduce_scatter | solution.py:265
  393.5 1.9 copy.244
  395.4 3.5 all-to-all-start.4
  399.0 8.6 %all-to-all-done.4 = bf16[4,128,512]{2,1,0:T(8,128)(2,1)S(1)} async-done(((bf16[4,128,512]{2,1,0:T(8,128)(2,1)}), bf16[4,128,512]{2,1,0:T(8,128)(2,1)S(1)}, u32[]{:S(2)}, u32[]{:S(2)}) %all-to-all-start.4) | async-done | bytes 524320 | tf_op jit(solution)/shard_map/all_to_all | solution.py:268
  407.7 1.2 gather_fusion.6
  408.9 0.8 multiply_reduce_fusion
  409.8 0.7 add_convert_fusion
  (123 shorter events, 11.1 us)
Async XLA Ops:
  6.5 44.1 %copy-start = (bf16[128,4096]{1,0:T(8,128)(2,1)S(1)}, bf16[128,4096]{1,0:T(8,128)(2,1)}, u32[]{:S(2)}) copy-start(bf16[128,4096]{1,0:T(8,128)(2,1)} %param.21) | copy-start | bytes 3145732
  6.5 53.3 %copy-start.8 = (s32[8,32]{1,0:T(8,128)S(1)}, s32[8,32]{1,0:T(8,128)}, u32[]{:S(2)}) copy-start(s32[8,32]{1,0:T(8,128)} %param.36) | copy-start | bytes 3076
  79.0 4.6 %copy-start.2 = (s32[32]{0:T(128)S(1)}, s32[32]{0:T(128)}, u32[]{:S(2)}) copy-start(s32[32]{0:T(128)} %param.39) | copy-start | bytes 388
  79.0 7.5 %copy-start.9 = (s32[32,4]{0,1:T(4,128)S(1)}, s32[32,4]{0,1:T(4,128)}, u32[]{:S(2)}) copy-start(s32[32,4]{0,1:T(4,128)} %param.37) | copy-start | bytes 1540
  110.0 4.7 %copy-start.10 = (s32[128]{0:T(128)S(1)}, s32[128]{0:T(128)}, u32[]{:S(2)}) copy-start(s32[128]{0:T(128)} %param.40) | copy-start | bytes 1540
  110.0 36.1 %all-to-all-start = ((f32[4,128,10,128]{1,3,2,0:T(8,128)}), f32[4,128,10,128]{1,3,2,0:T(8,128)}, u32[]{:S(2)}, u32[]{:S(2)}) async-start(f32[4,128,10,128]{1,3,2,0:T(8,128)} %copy.218), calls=%async_computation | async-start | bytes 5242880 | tf_op jit(solution)/shard_map/all_to_all | solution.py:149
  149.2 3.5 copy-start.3
  152.4 1.0 copy-start.4
  186.2 29.1 %all-to-all-start.2 = ((bf16[8,128,512]{2,1,0:T(8,128)(2,1)}), bf16[8,128,512]{2,1,0:T(8,128)(2,1)S(1)}, u32[]{:S(2)}, u32[]{:S(2)}) async-start(bf16[8,128,512]{2,1,0:T(8,128)(2,1)} %broadcast_in_dim.215), calls=%async_computation.2 | async-start | bytes 2097152 | tf_op jit(solution)/shard_map/all_to_all | solution.py:233
  189.7 203.8 %reduce-scatter.2.cloned.1.call-start = ((), (), s32[]{:S(2)}) async-start(), calls=%async_computation.6 | async-start | bytes 4718592 | tf_op jit(solution)/shard_map/reduce_scatter | solution.py:265
  189.8 26.3 %copy-start.6 = (f32[4096]{0:T(1024)S(1)}, f32[4096]{0:T(1024)}, u32[]{:S(2)}) copy-start(f32[4096]{0:T(1024)} %param.25) | copy-start | bytes 49156
  306.9 0.7 copy-start.7
  307.0 0.9 copy-start.5
  307.0 103.5 %copy-start.1 = (bf16[128,4096]{1,0:T(8,128)(2,1)S(1)}, bf16[128,4096]{1,0:T(8,128)(2,1)}, u32[]{:S(2)}) copy-start(bf16[128,4096]{1,0:T(8,128)(2,1)} %param.21) | copy-start | bytes 3145732
  395.4 12.3 %all-to-all-start.4 = ((bf16[4,128,512]{2,1,0:T(8,128)(2,1)}), bf16[4,128,512]{2,1,0:T(8,128)(2,1)S(1)}, u32[]{:S(2)}, u32[]{:S(2)}) async-start(bf16[4,128,512]{2,1,0:T(8,128)(2,1)} %bitcast.96), calls=%async_computation.5 | async-start | bytes 1048576 | tf_op jit(solution)/shard_map/all_to_all | solution.py:268
Sparse Core Ops, SparseCore 0:
  307.1 86.3 reduce-scatter.1
